TPU v7x, 1024 devices: a whole 8x8x8 slice. The times are simulated.
1024 devices in a mesh: box: 32 (over z, x_lo), param: 32 (over y, x_hi, core).
Axes of the slice: x: 8 (x_hi: 2, x_lo: 4; x = x_hi * 4 + x_lo), y: 8, z: 8, core: 2. Of those that a mesh axis runs over, the one named last changes fastest.
Arguments:
- traces: float32 [32, 32, 512, 256], P('box', 'param'), may hold values from -6 to 6
- owners: int32 [32, 32, 512, 1], P('box', 'param'), may hold values from 0 to 31; in each aligned block of 512 rows (0 to 511, 512 to 1023, ..., all dimensions but the last counted through in order) at most 32 rows name the same one
- counts: int32 [32, 32], P('box', 'param'), may hold values from 128 to 512, as said below
- pair_table: int32 [32, 32, 32, 32], P('box', 'param'), may hold values from 0 to 511
- anterp: float32 [256, 512], replicated, may hold values from -0.375 to 0.375
- interp: float32 [2, 512, 256], replicated, may hold values from -0.25 to 0.25
- phase: float32 [32, 32, 3, 512, 256], P('box', 'param'), may hold values from -3.140625 to 3.140625
Outputs:
- weights_out: float32 [32, 32, 2, 512, 256], P('box', 'param')
Inputs may be any that keep to these rules, and one draw needn't show every extreme that they name: `owners`: in the 512 rows of one device no owner is named more than 32 times, a bound that some block reaches. `counts`: some device has all 512 blocks live in every draw.
All inputs are finite; a program needn't handle non-finite values.
Results may differ from a plain program's by a relative error of at most 0.00011.
Values sent between devices are 32-bit elements; how exact they have to be, the bound alone decides.
No kernel may reach another device: no remote copies, remote signals or barrier semaphores. Data moves between devices by JAX's collectives and lax.ppermute only.
A program may use at most 32 MiB of HBM per device.

v0:
```python
import jax
import jax.numpy as jnp
from jax import lax
from jax.sharding import PartitionSpec as P

LEVELS = 3


HIGH = lax.Precision.HIGHEST


def swapped(x, axis, bit):
    return lax.ppermute(x, axis, [(i, i ^ 1 << bit) for i in range(lax.axis_size(axis))])


def rotate(weights_now, angles):
    cosine = jnp.cos(angles)
    sine_part = jnp.sin(angles)
    real_part = weights_now[0]
    imag_part = weights_now[1]
    return jnp.stack(
        [real_part * cosine - imag_part * sine_part, real_part * sine_part + imag_part * cosine],
        axis=0,
    )


def shards(traces, owners, counts, pair_table, anterp, interp, phase):
    blocks = traces[0, 0]
    destination = owners[0, 0, :, 0]
    live_count = counts[0, 0]
    param_count = lax.axis_size("param")
    slot_count = pair_table.shape[3]
    block_count = blocks.shape[0]
    weight_count = interp.shape[2]
    pair_count = phase.shape[3]
    live_mask = (jnp.arange(block_count, dtype=jnp.int32) < live_count).astype(jnp.float32)
    onehot = (destination[:, None] == jnp.arange(param_count, dtype=jnp.int32)[None, :]).astype(
        jnp.int32
    )
    ranking = jnp.sum((jnp.cumsum(onehot, axis=0) - onehot) * onehot, axis=1)
    position = destination * slot_count + ranking
    masked = blocks * live_mask[:, None]
    pair_ids = pair_table[0, 0].reshape(-1)
    selector = (jnp.arange(pair_count, dtype=jnp.int32)[:, None] == pair_ids[None, :]).astype(
        jnp.float32
    )
    coefficient = jnp.dot(masked, anterp, precision=HIGH)
    outgoing = (
        jnp.zeros((param_count * slot_count, 2 * weight_count), jnp.float32)
        .at[position]
        .set(coefficient)
    )
    arrived = lax.all_to_all(
        outgoing.reshape(param_count, slot_count, 2 * weight_count),
        "param",
        split_axis=0,
        concat_axis=0,
        tiled=True,
    )
    initial = jnp.dot(selector, arrived.reshape(-1, 2 * weight_count), precision=HIGH)
    weights_now = initial.reshape(pair_count, 2, weight_count).transpose(1, 0, 2)
    half_rows = pair_count // 2
    box_index = lax.axis_index("box")
    for level_id in range(LEVELS):
        side_bit = box_index >> level_id & 1
        kept_rows = lax.dynamic_slice_in_dim(weights_now, side_bit * half_rows, half_rows, 1)
        sent_rows = lax.dynamic_slice_in_dim(weights_now, (1 - side_bit) * half_rows, half_rows, 1)
        partner = swapped(sent_rows, "box", level_id)
        lower_rows = jnp.where(side_bit == 0, kept_rows, partner)
        upper_rows = jnp.where(side_bit == 0, partner, kept_rows)
        joined = jnp.concatenate([lower_rows, upper_rows], axis=2)
        combined = jnp.einsum("rqk,skj->rsqj", joined, interp, precision=HIGH).reshape(
            2, pair_count, weight_count
        )
        weights_now = rotate(combined, phase[0, 0, level_id])
    return weights_now[None, None]


def solution(mesh):
    placed = (
        P("box", "param", None, None),
        P("box", "param", None, None),
        P("box", "param"),
        P("box", "param", None, None),
        P(),
        P(),
        P("box", "param", None, None, None),
    )
    return jax.shard_map(
        shards,
        mesh=mesh,
        in_specs=placed,
        out_specs=P("box", "param", None, None, None),
        check_vma=False,
    )
```

profile of v0, /device:TPU:40, one launch (start us, length us, event | category | flops | bytes accessed | tf_op | source)
XLA Modules:
  0.0 169.5 jit_solution(2961653466449653716)
XLA Ops:
  0.0 0.0 copy-start
  0.0 0.8 fusion.30
  0.8 1.2 reduce-window.6
  1.9 0.2 slice_reduce_fusion
  2.2 0.8 fusion.29
  3.0 0.7 compare_select_fusion
  4.3 2.2 %fusion.25 = f32[512,512]{1,0:T(8,128)S(1)} fusion(f32[256,512]{1,0:T(8,128)} %param.11, f32[1,1,512,256]{3,2,1,0:T(8,128)} %param.7, f32[512]{0:T(512)S(1)} %fusion.31), kind=kOutput, calls=%fused_computation.56 | convolution fusion | flops 805437440 | bytes 2099200 | tf_op jit(solution)/shard_map/dot_general | solution.py:47
  6.6 3.7 %scatter_custom_fusion = f32[1024,512]{1,0:T(8,128)} fusion(s32[512]{0:T(512)S(1)} %bitcast.145, f32[512,512]{1,0:T(8,128)S(1)} %fusion.25, f32[]{:T(128)} %constant.9.clone.1), kind=kCustom, calls=%fused_computation.28 | custom fusion | bytes 2097156 | tf_op jit(solution)/shard_map/scatter | solution.py:51
  10.3 0.0 copy-start.1
  10.3 16.5 %all-to-all-start = ((f32[32,32,512]{2,1,0:T(8,128)}), f32[32,32,512]{2,1,0:T(8,128)S(1)}, u32[]{:S(2)}, u32[]{:S(2)}) async-start(f32[32,32,512]{2,1,0:T(8,128)} %bitcast.140), calls=%async_computation | async-start | bytes 4194304 | tf_op jit(solution)/shard_map/all_to_all | solution.py:53
  26.7 0.0 copy-done.1
  26.8 0.1 eq.56
  26.8 62.0 %all-to-all-done = f32[32,32,512]{2,1,0:T(8,128)S(1)} async-done(((f32[32,32,512]{2,1,0:T(8,128)}), f32[32,32,512]{2,1,0:T(8,128)S(1)}, u32[]{:S(2)}, u32[]{:S(2)}) %all-to-all-start) | async-done | bytes 2097184 | tf_op jit(solution)/shard_map/all_to_all | solution.py:53
  88.8 1.9 %copy.10 = f32[512,1024]{1,0:T(8,128)} copy(f32[512,1024]{0,1:T(8,128)S(1)} %bitcast.139) | data formatting | bytes 4194304 | tf_op jit(solution)/shard_map/dot_general | solution.py:60
  90.7 3.5 %fusion.1 = f32[512,2,256]{0,2,1:T(8,128)S(1)} fusion(f32[2,256,1024]{2,1,0:T(8,128)} %bitcast.141, s32[1024]{0:T(1024)S(1)} %eq.56), kind=kOutput, calls=%fused_computation.3 | convolution fusion | flops 3221749760 | bytes 3149824 | tf_op jit(solution)/shard_map/dot_general | solution.py:60
  94.3 1.9 %collective-permute-start = (f32[2,256,256]{1,2,0:T(8,128)S(1)}, f32[2,256,256]{1,2,0:T(8,128)S(1)}, u32[]{:S(2)}, u32[]{:S(2)}) collective-permute-start(f32[2,256,256]{1,2,0:T(8,128)S(1)} %dynamic-slice_bitcast_fusion), channel_id=1, source_target_pairs={{0,32},{32,0},{64,96},{96,64},{128,160},{160,128},{192,224},{224,1... | collective-permute-start | bytes 1572872 | tf_op jit(solution)/shard_map/ppermute | solution.py:13
  96.2 13.4 %collective-permute-done = f32[2,256,256]{1,2,0:T(8,128)S(1)} collective-permute-done((f32[2,256,256]{1,2,0:T(8,128)S(1)}, f32[2,256,256]{1,2,0:T(8,128)S(1)}, u32[]{:S(2)}, u32[]{:S(2)}) %collective-permute-start) | collective-permute-done | bytes 524320 | tf_op jit(solution)/shard_map/ppermute | solution.py:13
  109.7 0.1 bitcast_select_fusion.1
  109.8 0.0 copy-done
  109.8 1.9 %convolution_bitcast_fusion.2 = f32[2,2,256,256]{3,2,1,0:T(8,128)S(1)} fusion(f32[2,256,256]{1,2,0:T(8,128)S(1)} %get-tuple-element.16, f32[2,256,256]{1,2,0:T(8,128)S(1)} %get-tuple-element.15, f32[2,512,256]{2,1,0:T(8,128)S(1)} %copy-done), kind=kOutput, calls=%fused_computation.6 | convolution fusion | flops 1610874880 | bytes 3145728 | tf_op jit(solution)/shard_map/rqk,skj->rsqj/dot_general | solution.py:72
  111.6 0.1 fusion.37
  111.7 3.4 %fusion.24 = (f32[1,512,256]{2,1,0:T(8,128)S(1)}, f32[1,512,256]{2,1,0:T(8,128)S(1)}) fusion(f32[1,2,256,256]{3,2,1,0:T(8,128)S(1)} %get-tuple-element.22, f32[1,2,256,256]{3,2,1,0:T(8,128)S(1)} %get-tuple-element.21, f32[1,1,3,512,256]{4,3,2,1,0:T(8,128)} %param.13), kind=kLoop, calls=%fused_computation.50 | loop fusion | flops 786432 | bytes 2621440 | tf_op jit(solution)/shard_map/add | solution.py:22
  115.2 1.9 %collective-permute-start.1 = (f32[2,256,256]{2,1,0:T(8,128)S(1)}, f32[2,256,256]{2,1,0:T(8,128)S(1)}, u32[]{:S(2)}, u32[]{:S(2)}) collective-permute-start(f32[2,256,256]{2,1,0:T(8,128)S(1)} %fusion.17), channel_id=1, source_target_pairs={{0,64},{32,96},{64,0},{96,32},{128,192},{160,224},{192,128},{224,1... | collective-permute-start | bytes 1572872 | tf_op jit(solution)/shard_map/ppermute | solution.py:13
  117.1 24.7 %collective-permute-done.1 = f32[2,256,256]{2,1,0:T(8,128)S(1)} collective-permute-done((f32[2,256,256]{2,1,0:T(8,128)S(1)}, f32[2,256,256]{2,1,0:T(8,128)S(1)}, u32[]{:S(2)}, u32[]{:S(2)}) %collective-permute-start.1) | collective-permute-done | bytes 524320 | tf_op jit(solution)/shard_map/ppermute | solution.py:13
  141.8 0.1 broadcast_select_fusion.1
  141.9 1.8 %convolution_bitcast_fusion.1 = f32[2,2,256,256]{3,2,1,0:T(8,128)S(1)} fusion(f32[2,256,256]{2,1,0:T(8,128)S(1)} %get-tuple-element.14, f32[2,256,256]{2,1,0:T(8,128)S(1)} %get-tuple-element.13, f32[2,512,256]{2,1,0:T(8,128)S(1)} %copy-done), kind=kOutput, calls=%fused_computation.5 | convolution fusion | flops 1610874880 | bytes 3145728 | tf_op jit(solution)/shard_map/rqk,skj->rsqj/dot_general | solution.py:72
  143.8 0.1 fusion.36
  143.8 3.4 %fusion.22 = (f32[1,512,256]{2,1,0:T(8,128)S(1)}, f32[1,512,256]{2,1,0:T(8,128)S(1)}) fusion(f32[1,2,256,256]{3,2,1,0:T(8,128)S(1)} %get-tuple-element.20, f32[1,2,256,256]{3,2,1,0:T(8,128)S(1)} %get-tuple-element.19, f32[1,1,3,512,256]{4,3,2,1,0:T(8,128)} %param.13), kind=kLoop, calls=%fused_computation.44 | loop fusion | flops 786432 | bytes 2621440 | tf_op jit(solution)/shard_map/add | solution.py:22
  147.3 2.1 %collective-permute-start.2 = (f32[2,256,256]{2,1,0:T(8,128)S(1)}, f32[2,256,256]{2,1,0:T(8,128)S(1)}, u32[]{:S(2)}, u32[]{:S(2)}) collective-permute-start(f32[2,256,256]{2,1,0:T(8,128)S(1)} %fusion.15), channel_id=1, source_target_pairs={{0,128},{32,160},{64,192},{96,224},{128,0},{160,32},{192,64},{224,... | collective-permute-start | bytes 1572872 | tf_op jit(solution)/shard_map/ppermute | solution.py:13
  149.4 13.6 %collective-permute-done.2 = f32[2,256,256]{2,1,0:T(8,128)S(1)} collective-permute-done((f32[2,256,256]{2,1,0:T(8,128)S(1)}, f32[2,256,256]{2,1,0:T(8,128)S(1)}, u32[]{:S(2)}, u32[]{:S(2)}) %collective-permute-start.2) | collective-permute-done | bytes 524320 | tf_op jit(solution)/shard_map/ppermute | solution.py:13
  163.0 0.1 broadcast_select_fusion.3
  163.1 1.8 %convolution_bitcast_fusion = f32[2,2,256,256]{3,2,1,0:T(8,128)S(1)} fusion(f32[2,256,256]{2,1,0:T(8,128)S(1)} %get-tuple-element.12, f32[2,256,256]{2,1,0:T(8,128)S(1)} %get-tuple-element.11, f32[2,512,256]{2,1,0:T(8,128)S(1)} %copy-done), kind=kOutput, calls=%fused_computation.4 | convolution fusion | flops 1610874880 | bytes 3145728 | tf_op jit(solution)/shard_map/rqk,skj->rsqj/dot_general | solution.py:72
  164.9 0.1 fusion.35
  165.0 3.4 %fusion.19 = (f32[1,512,256]{2,1,0:T(8,128)S(1)}, f32[1,512,256]{2,1,0:T(8,128)S(1)}) fusion(f32[1,2,256,256]{3,2,1,0:T(8,128)S(1)} %get-tuple-element.18, f32[1,2,256,256]{3,2,1,0:T(8,128)S(1)} %get-tuple-element.17, f32[1,1,3,512,256]{4,3,2,1,0:T(8,128)} %param.13), kind=kLoop, calls=%fused_computation.37 | loop fusion | flops 786432 | bytes 2621440 | tf_op jit(solution)/shard_map/sub | solution.py:22
  168.4 1.0 maximum_bitcast_fusion.6
  (6 shorter events, 0.2 us)
Async XLA Ops:
  0.0 109.8 %copy-start = (f32[2,512,256]{2,1,0:T(8,128)S(1)}, f32[2,512,256]{2,1,0:T(8,128)}, u32[]{:S(2)}) copy-start(f32[2,512,256]{2,1,0:T(8,128)} %param.12) | copy-start | bytes 3145732
  10.3 16.5 %copy-start.1 = (s32[1,1,32,32]{3,2,1,0:T(8,128)S(1)}, s32[1,1,32,32]{3,2,1,0:T(8,128)}, u32[]{:S(2)}) copy-start(s32[1,1,32,32]{3,2,1,0:T(8,128)} %param.10) | copy-start | bytes 12292
  10.3 78.6 %all-to-all-start = ((f32[32,32,512]{2,1,0:T(8,128)}), f32[32,32,512]{2,1,0:T(8,128)S(1)}, u32[]{:S(2)}, u32[]{:S(2)}) async-start(f32[32,32,512]{2,1,0:T(8,128)} %bitcast.140), calls=%async_computation | async-start | bytes 4194304 | tf_op jit(solution)/shard_map/all_to_all | solution.py:53
  94.3 15.4 %collective-permute-start = (f32[2,256,256]{1,2,0:T(8,128)S(1)}, f32[2,256,256]{1,2,0:T(8,128)S(1)}, u32[]{:S(2)}, u32[]{:S(2)}) collective-permute-start(f32[2,256,256]{1,2,0:T(8,128)S(1)} %dynamic-slice_bitcast_fusion), channel_id=1, source_target_pairs={{0,32},{32,0},{64,96},{96,64},{128,160},{160,128},{192,224},{224,1... | collective-permute-start | bytes 1572872 | tf_op jit(solution)/shard_map/ppermute | solution.py:13
  115.2 26.7 %collective-permute-start.1 = (f32[2,256,256]{2,1,0:T(8,128)S(1)}, f32[2,256,256]{2,1,0:T(8,128)S(1)}, u32[]{:S(2)}, u32[]{:S(2)}) collective-permute-start(f32[2,256,256]{2,1,0:T(8,128)S(1)} %fusion.17), channel_id=1, source_target_pairs={{0,64},{32,96},{64,0},{96,32},{128,192},{160,224},{192,128},{224,1... | collective-permute-start | bytes 1572872 | tf_op jit(solution)/shard_map/ppermute | solution.py:13
  147.3 15.7 %collective-permute-start.2 = (f32[2,256,256]{2,1,0:T(8,128)S(1)}, f32[2,256,256]{2,1,0:T(8,128)S(1)}, u32[]{:S(2)}, u32[]{:S(2)}) collective-permute-start(f32[2,256,256]{2,1,0:T(8,128)S(1)} %fusion.15), channel_id=1, source_target_pairs={{0,128},{32,160},{64,192},{96,224},{128,0},{160,32},{192,64},{224,... | collective-permute-start | bytes 1572872 | tf_op jit(solution)/shard_map/ppermute | solution.py:13
where the time goes:
time: 170 us; the launch traced here: 169 us
  waiting for transfers between devices  114 us (67%)
  starting transfers between devices  22.4 us (13%)
  other arithmetic  15 us (9%)
  matrix products  11.3 us (7%)
  local copies, waits for them, and re-layouts  6.1 us (4%)
    all_to_all x1, waiting for transfers between devices, shards(): lax.all_to_all(outgoing.reshape(param_count, slot_count, 2 * weight_count...  62 us
    ppermute x3, waiting for transfers between devices, swapped(): lax.ppermute(x, axis, [(i, i ^ 1 << bit) for i in range(lax.axis_size(axi...  51.8 us
    all_to_all x1, starting transfers between devices, shards(): lax.all_to_all(outgoing.reshape(param_count, slot_count, 2 * weight_count...  16.5 us
    add x2, other arithmetic, rotate(): real_part * sine_part + imag_part * cosine  6.75 us
    ppermute x3, starting transfers between devices, swapped(): lax.ppermute(x, axis, [(i, i ^ 1 << bit) for i in range(lax.axis_size(axi...  5.94 us
    dot_general x3, matrix products, shards(): jnp.einsum('rqk,skj->rsqj', joined, interp, precision=HIGH)  5.54 us
    scatter x1, local copies, waits for them, and re-layouts, shards(): outgoing = jnp.zeros((param_count * slot_count, 2 * weight_count), jnp.fl...  3.67 us
    dot_general x1, matrix products, shards(): jnp.dot(selector, arrived.reshape(-1, 2 * weight_count), precision=HIGH)  3.55 us
  transfers between devices with their start and end apart: 4, of which 4 were waited for; matrix products, arithmetic and copies ran while one was open for 0% of the time, Pallas kernels for 0%

commit v1 on v0

--- a/solution.py
+++ b/solution.py
@@ -13,9 +13,7 @@
     return lax.ppermute(x, axis, [(i, i ^ 1 << bit) for i in range(lax.axis_size(axis))])
 
 
-def rotate(weights_now, angles):
-    cosine = jnp.cos(angles)
-    sine_part = jnp.sin(angles)
+def rotate(weights_now, cosine, sine_part):
     real_part = weights_now[0]
     imag_part = weights_now[1]
     return jnp.stack(
@@ -31,6 +29,7 @@
     param_count = lax.axis_size("param")
     slot_count = pair_table.shape[3]
     block_count = blocks.shape[0]
+    trace_count = blocks.shape[1]
     weight_count = interp.shape[2]
     pair_count = phase.shape[3]
     live_mask = (jnp.arange(block_count, dtype=jnp.int32) < live_count).astype(jnp.float32)
@@ -44,21 +43,22 @@
     selector = (jnp.arange(pair_count, dtype=jnp.int32)[:, None] == pair_ids[None, :]).astype(
         jnp.float32
     )
-    coefficient = jnp.dot(masked, anterp, precision=HIGH)
     outgoing = (
-        jnp.zeros((param_count * slot_count, 2 * weight_count), jnp.float32)
-        .at[position]
-        .set(coefficient)
+        jnp.zeros((param_count * slot_count, trace_count), jnp.float32).at[position].set(masked)
     )
     arrived = lax.all_to_all(
-        outgoing.reshape(param_count, slot_count, 2 * weight_count),
+        outgoing.reshape(param_count, slot_count, trace_count),
         "param",
         split_axis=0,
         concat_axis=0,
         tiled=True,
     )
-    initial = jnp.dot(selector, arrived.reshape(-1, 2 * weight_count), precision=HIGH)
-    weights_now = initial.reshape(pair_count, 2, weight_count).transpose(1, 0, 2)
+    angles = phase[0, 0]
+    cosines, sines = lax.optimization_barrier((jnp.cos(angles), jnp.sin(angles)))
+    gathered = jnp.dot(selector, arrived.reshape(-1, trace_count), precision=HIGH)
+    weights_now = jnp.einsum(
+        "pt,trk->rpk", gathered, anterp.reshape(trace_count, 2, weight_count), precision=HIGH
+    )
     half_rows = pair_count // 2
     box_index = lax.axis_index("box")
     for level_id in range(LEVELS):
@@ -72,7 +72,7 @@
         combined = jnp.einsum("rqk,skj->rsqj", joined, interp, precision=HIGH).reshape(
             2, pair_count, weight_count
         )
-        weights_now = rotate(combined, phase[0, 0, level_id])
+        weights_now = rotate(combined, cosines[level_id], sines[level_id])
     return weights_now[None, None]
 
 

time: 170 us -> 134 us (0.79)
  the two profiles are of different devices: /device:TPU:40 before, /device:TPU:8 now
where the time goes in v1:
time: 134 us; the launch traced here: 133 us
  waiting for transfers between devices  73.2 us (55%)
  starting transfers between devices  22.4 us (17%)
  other arithmetic  17.6 us (13%)
  local copies, waits for them, and re-layouts  11.5 us (9%)
  matrix products  7.81 us (6%)
    ppermute x3, waiting for transfers between devices, swapped(): lax.ppermute(x, axis, [(i, i ^ 1 << bit) for i in range(lax.axis_size(axi...  44.6 us
    all_to_all x1, waiting for transfers between devices, shards(): lax.all_to_all(outgoing.reshape(param_count, slot_count, trace_count), 'p...  28.6 us
    all_to_all x1, starting transfers between devices, shards(): lax.all_to_all(outgoing.reshape(param_count, slot_count, trace_count), 'p...  16.7 us
    sin x1, local copies, waits for them, and re-layouts, shards(): jnp.sin(angles)  8.15 us
    ppermute x3, starting transfers between devices, swapped(): lax.ppermute(x, axis, [(i, i ^ 1 << bit) for i in range(lax.axis_size(axi...  5.74 us
    dot_general x3, matrix products, shards(): jnp.einsum('rqk,skj->rsqj', joined, interp, precision=HIGH)  5.54 us
    scatter x1, other arithmetic, shards(): jnp.zeros((param_count * slot_count, trace_count), jnp.float32).at[position]  3.89 us
    select_n x3, other arithmetic, shards(): lower_rows = jnp.where(side_bit == 0, kept_rows, partner)  3.87 us
  transfers between devices with their start and end apart: 4, of which 4 were waited for; matrix products, arithmetic and copies ran while one was open for 6% of the time, Pallas kernels for 0%

profile of v1, /device:TPU:8, one launch (start us, length us, event | category | flops | bytes accessed | tf_op | source)
XLA Modules:
  0.0 133.4 jit_solution(8429144295695430244)
XLA Ops:
  0.0 0.0 copy-start
  0.0 0.8 fusion.28
  0.8 1.2 reduce-window.6
  1.9 0.2 slice_reduce_fusion
  2.2 0.8 fusion.27
  3.0 0.7 compare_select_fusion
  4.3 0.0 copy-start.5
  4.4 0.0 copy-start.4
  4.4 3.9 %scatter_custom_fusion = f32[1024,256]{1,0:T(8,128)} fusion(s32[512]{0:T(512)S(1)} %bitcast.128, f32[1,1,512,256]{3,2,1,0:T(8,128)} %param.7, f32[]{:T(128)} %constant.9.clone.1, f32[512]{0:T(512)S(1)} %fusion.29), kind=kCustom, calls=%fused_computation.56 | custom fusion | flops 131072 | bytes 1574916 | tf_op jit(solution)/shard_map/scatter | solution.py:47
  8.3 16.7 %all-to-all-start = ((f32[32,32,256]{2,1,0:T(8,128)}), f32[32,32,256]{2,1,0:T(8,128)S(1)}, u32[]{:S(2)}, u32[]{:S(2)}) async-start(f32[32,32,256]{2,1,0:T(8,128)} %bitcast.8), calls=%async_computation | async-start | bytes 2097152 | tf_op jit(solution)/shard_map/all_to_all | solution.py:49
  24.9 0.0 copy-done.5
  25.0 0.1 eq.56
  25.0 0.0 copy-done.4
  25.0 0.2 copy.16
  25.2 28.6 %all-to-all-done = f32[32,32,256]{2,1,0:T(8,128)S(1)} async-done(((f32[32,32,256]{2,1,0:T(8,128)}), f32[32,32,256]{2,1,0:T(8,128)S(1)}, u32[]{:S(2)}, u32[]{:S(2)}) %all-to-all-start) | async-done | bytes 1048608 | tf_op jit(solution)/shard_map/all_to_all | solution.py:49
  53.9 1.2 fusion.1
  55.1 1.0 fusion.36
  56.2 0.0 copy-start.3
  56.2 1.0 copy-done.3
  57.2 1.9 %collective-permute-start = (f32[2,256,256]{1,2,0:T(8,128)S(1)}, f32[2,256,256]{1,2,0:T(8,128)}, u32[]{:S(2)}, u32[]{:S(2)}) collective-permute-start(f32[2,256,256]{1,2,0:T(8,128)S(1)} %dynamic-slice_bitcast_fusion), channel_id=1, source_target_pairs={{0,32},{32,0},{64,96},{96,64},{128,160},{160,128},{192,224},{224,1... | collective-permute-start | bytes 1572872 | tf_op jit(solution)/shard_map/ppermute | solution.py:13
  59.1 8.2 %sine_bitcast_fusion = (f32[3,512,256]{2,1,0:T(8,128)S(1)}, f32[3,512,256]{2,1,0:T(8,128)}) fusion(f32[1,1,3,512,256]{4,3,2,1,0:T(8,128)} %param.13), kind=kLoop, calls=%fused_computation.3 | loop fusion | bytes 4718592 | tf_op jit(solution)/shard_map/sin | solution.py:57
  67.3 5.4 %collective-permute-done = f32[2,256,256]{1,2,0:T(8,128)} collective-permute-done((f32[2,256,256]{1,2,0:T(8,128)S(1)}, f32[2,256,256]{1,2,0:T(8,128)}, u32[]{:S(2)}, u32[]{:S(2)}) %collective-permute-start) | collective-permute-done | bytes 524320 | tf_op jit(solution)/shard_map/ppermute | solution.py:13
  72.7 1.3 bitcast_select_fusion.1
  74.0 0.0 copy-done
  74.0 1.9 %convolution_bitcast_fusion.2 = f32[2,2,256,256]{3,2,1,0:T(8,128)S(1)} fusion(f32[2,256,256]{1,2,0:T(8,128)S(1)} %get-tuple-element.22, f32[2,256,256]{1,2,0:T(8,128)S(1)} %get-tuple-element.21, f32[2,512,256]{2,1,0:T(8,128)S(1)} %copy-done), kind=kOutput, calls=%fused_computation.7 | convolution fusion | flops 1610874880 | bytes 3145728 | tf_op jit(solution)/shard_map/rqk,skj->rsqj/dot_general | solution.py:72
  75.8 0.1 fusion.35
  75.9 1.2 fusion.21
  77.2 0.0 copy-start.1
  77.2 0.8 copy-done.1
  78.0 0.8 fusion.14
  78.8 1.9 %collective-permute-start.1 = (f32[2,256,256]{2,1,0:T(8,128)}, f32[2,256,256]{2,1,0:T(8,128)}, u32[]{:S(2)}, u32[]{:S(2)}) collective-permute-start(f32[2,256,256]{2,1,0:T(8,128)} %fusion.14), channel_id=1, source_target_pairs={{0,64},{32,96},{64,0},{96,32},{128,192},{160,224},{192,128},{224,1... | collective-permute-start | bytes 1572872 | tf_op jit(solution)/shard_map/ppermute | solution.py:13
  80.7 25.1 %collective-permute-done.1 = f32[2,256,256]{2,1,0:T(8,128)} collective-permute-done((f32[2,256,256]{2,1,0:T(8,128)}, f32[2,256,256]{2,1,0:T(8,128)}, u32[]{:S(2)}, u32[]{:S(2)}) %collective-permute-start.1) | collective-permute-done | bytes 524320 | tf_op jit(solution)/shard_map/ppermute | solution.py:13
  105.8 1.3 broadcast_select_fusion.1
  107.1 1.8 %convolution_bitcast_fusion.1 = f32[2,2,256,256]{3,2,1,0:T(8,128)S(1)} fusion(f32[2,256,256]{2,1,0:T(8,128)S(1)} %get-tuple-element.18, f32[2,256,256]{2,1,0:T(8,128)S(1)} %get-tuple-element.17, f32[2,512,256]{2,1,0:T(8,128)S(1)} %copy-done), kind=kOutput, calls=%fused_computation.6 | convolution fusion | flops 1610874880 | bytes 3145728 | tf_op jit(solution)/shard_map/rqk,skj->rsqj/dot_general | solution.py:72
  108.9 0.1 fusion.34
  109.0 1.2 fusion.19
  110.3 0.0 copy-start.2
  110.3 0.8 copy-done.2
  111.1 0.8 fusion.12
  111.9 1.9 %collective-permute-start.2 = (f32[2,256,256]{2,1,0:T(8,128)}, f32[2,256,256]{2,1,0:T(8,128)}, u32[]{:S(2)}, u32[]{:S(2)}) collective-permute-start(f32[2,256,256]{2,1,0:T(8,128)} %fusion.12), channel_id=1, source_target_pairs={{0,128},{32,160},{64,192},{96,224},{128,0},{160,32},{192,64},{224,... | collective-permute-start | bytes 1572872 | tf_op jit(solution)/shard_map/ppermute | solution.py:13
  113.8 14.1 %collective-permute-done.2 = f32[2,256,256]{2,1,0:T(8,128)} collective-permute-done((f32[2,256,256]{2,1,0:T(8,128)}, f32[2,256,256]{2,1,0:T(8,128)}, u32[]{:S(2)}, u32[]{:S(2)}) %collective-permute-start.2) | collective-permute-done | bytes 524320 | tf_op jit(solution)/shard_map/ppermute | solution.py:13
  127.9 1.3 broadcast_select_fusion.3
  129.2 1.8 %convolution_bitcast_fusion = f32[2,2,256,256]{3,2,1,0:T(8,128)S(1)} fusion(f32[2,256,256]{2,1,0:T(8,128)S(1)} %get-tuple-element.16, f32[2,256,256]{2,1,0:T(8,128)S(1)} %get-tuple-element.15, f32[2,512,256]{2,1,0:T(8,128)S(1)} %copy-done), kind=kOutput, calls=%fused_computation.5 | convolution fusion | flops 1610874880 | bytes 3145728 | tf_op jit(solution)/shard_map/rqk,skj->rsqj/dot_general | solution.py:72
  131.1 0.1 fusion.33
  131.2 1.2 fusion.16
  132.4 1.0 maximum_bitcast_fusion.6
  (4 shorter events, 0.1 us)
Async XLA Ops:
  0.0 74.0 %copy-start = (f32[2,512,256]{2,1,0:T(8,128)S(1)}, f32[2,512,256]{2,1,0:T(8,128)}, u32[]{:S(2)}) copy-start(f32[2,512,256]{2,1,0:T(8,128)} %param.12) | copy-start | bytes 3145732
  4.3 20.6 %copy-start.5 = (s32[1,1,32,32]{3,2,1,0:T(8,128)S(1)}, s32[1,1,32,32]{3,2,1,0:T(8,128)}, u32[]{:S(2)}) copy-start(s32[1,1,32,32]{3,2,1,0:T(8,128)} %param.10) | copy-start | bytes 12292
  4.4 20.7 %copy-start.4 = (f32[256,512]{1,0:T(8,128)S(1)}, f32[256,512]{1,0:T(8,128)}, u32[]{:S(2)}) copy-start(f32[256,512]{1,0:T(8,128)} %param.11) | copy-start | bytes 1572868
  8.3 45.6 %all-to-all-start = ((f32[32,32,256]{2,1,0:T(8,128)}), f32[32,32,256]{2,1,0:T(8,128)S(1)}, u32[]{:S(2)}, u32[]{:S(2)}) async-start(f32[32,32,256]{2,1,0:T(8,128)} %bitcast.8), calls=%async_computation | async-start | bytes 2097152 | tf_op jit(solution)/shard_map/all_to_all | solution.py:49
  56.2 1.0 copy-start.3
  57.2 15.5 %collective-permute-start = (f32[2,256,256]{1,2,0:T(8,128)S(1)}, f32[2,256,256]{1,2,0:T(8,128)}, u32[]{:S(2)}, u32[]{:S(2)}) collective-permute-start(f32[2,256,256]{1,2,0:T(8,128)S(1)} %dynamic-slice_bitcast_fusion), channel_id=1, source_target_pairs={{0,32},{32,0},{64,96},{96,64},{128,160},{160,128},{192,224},{224,1... | collective-permute-start | bytes 1572872 | tf_op jit(solution)/shard_map/ppermute | solution.py:13
  77.2 0.8 copy-start.1
  78.8 27.0 %collective-permute-start.1 = (f32[2,256,256]{2,1,0:T(8,128)}, f32[2,256,256]{2,1,0:T(8,128)}, u32[]{:S(2)}, u32[]{:S(2)}) collective-permute-start(f32[2,256,256]{2,1,0:T(8,128)} %fusion.14), channel_id=1, source_target_pairs={{0,64},{32,96},{64,0},{96,32},{128,192},{160,224},{192,128},{224,1... | collective-permute-start | bytes 1572872 | tf_op jit(solution)/shard_map/ppermute | solution.py:13
  110.3 0.8 copy-start.2
  111.9 16.0 %collective-permute-start.2 = (f32[2,256,256]{2,1,0:T(8,128)}, f32[2,256,256]{2,1,0:T(8,128)}, u32[]{:S(2)}, u32[]{:S(2)}) collective-permute-start(f32[2,256,256]{2,1,0:T(8,128)} %fusion.12), channel_id=1, source_target_pairs={{0,128},{32,160},{64,192},{96,224},{128,0},{160,32},{192,64},{224,... | collective-permute-start | bytes 1572872 | tf_op jit(solution)/shard_map/ppermute | solution.py:13
